TPU v7x, 512 devices: a whole 4x8x8 slice. The times are simulated.
512 devices in a mesh: group: 16 (over x_lo, z), row: 32 (over x_hi, y, core).
Axes of the slice: x: 4 (x_hi: 2, x_lo: 2; x = x_hi * 2 + x_lo), y: 8, z: 8, core: 2. Of those that a mesh axis runs over, the one named last changes fastest.
Arguments:
- features: float32 [98304, 2048], P('row', 'group'), may hold values from -6 to 6
- feature_id: int32 [2048], P('group'), may hold values from 0 to 2047, each once
- feature_shift: float32 [2048], replicated, may hold values from -3 to 3
- feature_scale: float32 [2048], replicated, may hold values from 0.25 to 2
- proj_weight: bfloat16 [2048, 256], P('group'), may hold values from -0.5 to 0.5
- row_slot: int32 [32, 3072], P('row'), may hold values from 0 to 3071, each once within a row
- down_weight: bfloat16 [2, 4096, 128], P(None, 'row'), may hold values from -0.09375 to 0.09375
- up_weight: bfloat16 [2, 4096, 128], P(None, 'row'), may hold values from -0.5 to 0.5
- cross_bias: float32 [2, 4096], replicated, may hold values from -3 to 3
- head_weight: float32 [4096], replicated, may hold values from -0.09375 to 0.09375
- labels: int32 [98304], P(('group', 'row')), may hold values 0 or 1
Outputs:
- logits: float32 [98304], P(('group', 'row'))
- grad_down: float32 [2, 4096, 128], P(None, 'row')
- grad_up: float32 [2, 4096, 128], P(None, 'row')
- grad_bias: float32 [2, 4096], replicated
- grad_proj: float32 [2048, 256], P('group')
Inputs may be any that keep to these rules, and one draw needn't show every extreme that they name: Each row of row_slot holds every number 0 .. 3071 once. feature_id holds every number 0 .. 2047 once.
All inputs are finite; a program needn't handle non-finite values. No bound on the sum of `labels` on one device may be relied on, other than what follows from the above.
Results may differ from a plain program's by a relative error of at most 0.02.
Values may be sent and summed in bfloat16 or wider, within the bound.
No kernel may reach another device: no remote copies, remote signals or barrier semaphores. Data moves between devices by JAX's collectives and lax.ppermute only.
A program may use at most 64 MiB of HBM per device.

v0:
```python
import jax
import jax.numpy as jnp
from jax import lax
from jax.sharding import PartitionSpec as P


def column_table(feature_id, lookup_table):
    columns = jnp.arange(lookup_table.shape[0], dtype=jnp.int32)
    picker = (feature_id[:, None] == columns[None, :]).astype(jnp.float32)
    return jnp.dot(picker, lookup_table, precision=lax.Precision.HIGHEST)


def exchange_sum(partial, axis, count):
    pieces = partial.reshape(count, -1)
    mine = jnp.sum(lax.all_to_all(pieces, axis, 0, 0, tiled=True), axis=0)
    spread = jnp.broadcast_to(mine[None], pieces.shape)
    return lax.all_to_all(spread, axis, 0, 0, tiled=True).reshape(partial.shape)


def group_all_reduce(rows, groups):
    stacked, height, width = rows.shape
    pieces = rows.reshape(stacked, groups, height // groups, width).transpose(1, 0, 2, 3)
    mine = jnp.sum(lax.all_to_all(pieces, "group", 0, 0, tiled=True).astype(jnp.float32), axis=0)
    spread = jnp.broadcast_to(mine.astype(jnp.bfloat16)[None], pieces.shape)
    gathered = lax.all_to_all(spread, "group", 0, 0, tiled=True).astype(jnp.float32)
    return gathered.transpose(1, 0, 2, 3).reshape(rows.shape)


def body(
    features,
    feature_id,
    feature_shift,
    feature_scale,
    proj_weight,
    row_slot,
    down_weight,
    up_weight,
    cross_bias,
    head_weight,
    labels,
):
    layers = down_weight.shape[0]
    groups = lax.axis_size("group")
    row_count = labels.shape[0]
    feature_stats = column_table(feature_id, jnp.stack([feature_shift, feature_scale], axis=1))
    normed = ((features - feature_stats[:, 0][None, :]) * feature_stats[:, 1][None, :]).astype(
        jnp.bfloat16
    )
    ordered = jnp.zeros_like(normed).at[row_slot[0]].set(normed)
    projected = jnp.dot(ordered, proj_weight, preferred_element_type=jnp.float32).astype(
        jnp.bfloat16
    )
    first = lax.all_to_all(projected, "group", split_axis=0, concat_axis=1, tiled=True)
    first_wide = first.astype(jnp.float32)
    crossed = first
    stored = []
    weights_full = lax.all_gather(
        jnp.concatenate([down_weight, up_weight], axis=0), "row", axis=1, tiled=True
    )
    for layer_index in range(layers):
        down_full, up_full = (weights_full[layer_index], weights_full[layers + layer_index])
        hidden = jnp.dot(crossed, down_full, preferred_element_type=jnp.float32).astype(
            jnp.bfloat16
        )
        mixture = lax.dot_general(
            hidden, up_full, (((1,), (1,)), ((), ())), preferred_element_type=jnp.float32
        )
        mixture = mixture + cross_bias[layer_index][None, :]
        stored.append((crossed, hidden, mixture, down_full, up_full))
        crossed = (first_wide * mixture + crossed.astype(jnp.float32)).astype(jnp.bfloat16)
    logits = jnp.sum(crossed.astype(jnp.float32) * head_weight[None, :], axis=1)
    total_rows = row_count * groups * lax.axis_size("row")
    loss_scale = 2.0 * (crossed.shape[1] / total_rows) ** 0.5
    logit_grad = (jax.nn.sigmoid(logits) - labels.astype(jnp.float32)) * loss_scale
    back = (logit_grad[:, None] * head_weight[None, :]).astype(jnp.bfloat16)
    first_grad = jnp.zeros(first.shape, jnp.float32)
    up_parts = [None] * layers
    down_parts = [None] * layers
    bias_terms = [None] * layers
    for layer_index in reversed(range(layers)):
        crossed_in, hidden, mixture, down_full, up_full = stored[layer_index]
        back_wide = back.astype(jnp.float32)
        first_grad = first_grad + back_wide * mixture
        mix_grad = (back_wide * first_wide).astype(jnp.bfloat16)
        up_term = lax.dot_general(
            mix_grad, hidden, (((0,), (0,)), ((), ())), preferred_element_type=jnp.float32
        )
        bias_terms[layer_index] = mix_grad
        hidden_grad = jnp.dot(mix_grad, up_full, preferred_element_type=jnp.float32).astype(
            jnp.bfloat16
        )
        down_term = lax.dot_general(
            crossed_in, hidden_grad, (((0,), (0,)), ((), ())), preferred_element_type=jnp.float32
        )
        through = lax.dot_general(
            hidden_grad, down_full, (((1,), (1,)), ((), ())), preferred_element_type=jnp.float32
        )
        back = (back_wide + through).astype(jnp.bfloat16)
        up_parts[layer_index] = up_term
        down_parts[layer_index] = down_term
    slab = jnp.stack(up_parts + down_parts).astype(jnp.bfloat16)
    slab, bias_terms = lax.optimization_barrier((slab, bias_terms))
    bias_terms = [jnp.sum(mix_grad.astype(jnp.float32), axis=0) for mix_grad in bias_terms]
    weight_rows = lax.psum_scatter(slab, "row", scatter_dimension=1, tiled=True)
    first_grad = (first_grad + back.astype(jnp.float32)).astype(jnp.bfloat16)
    owner_grad = lax.all_to_all(first_grad, "group", split_axis=1, concat_axis=0, tiled=True)
    proj_term = lax.dot_general(
        ordered, owner_grad, (((0,), (0,)), ((), ())), preferred_element_type=jnp.float32
    )
    row_count_axis = lax.axis_size("row")
    bias_all = jnp.stack(bias_terms)
    proj_pieces = proj_term.reshape(row_count_axis, -1)
    bias_pieces = bias_all.reshape(layers, row_count_axis, -1).transpose(1, 0, 2)
    bias_pieces = bias_pieces.reshape(row_count_axis, -1)
    split = proj_pieces.shape[1]
    row_mine = jnp.sum(
        lax.all_to_all(
            jnp.concatenate([proj_pieces, bias_pieces], axis=1), "row", 0, 0, tiled=True
        ),
        axis=0,
    )
    bias_chunk = exchange_sum(row_mine[split:], "group", groups)
    last = jnp.concatenate([row_mine[:split], bias_chunk])
    last_all = lax.all_to_all(
        jnp.broadcast_to(last[None], (row_count_axis,) + last.shape), "row", 0, 0, tiled=True
    )
    grad_proj = last_all[:, :split].reshape(proj_term.shape)
    grad_bias = (
        last_all[:, split:]
        .reshape(row_count_axis, layers, -1)
        .transpose(1, 0, 2)
        .reshape(bias_all.shape)
    )
    weight_rows, grad_proj, grad_bias = lax.optimization_barrier(
        (weight_rows, grad_proj, grad_bias)
    )
    weight_sums = group_all_reduce(weight_rows, groups)
    grad_up, grad_down = (weight_sums[:layers], weight_sums[layers:])
    return (logits, grad_down, grad_up, grad_bias, grad_proj)


def solution(mesh):
    in_specs = (
        P("row", "group"),
        P("group"),
        P(),
        P(),
        P("group", None),
        P("row", None),
        P(None, "row", None),
        P(None, "row", None),
        P(),
        P(),
        P(("group", "row")),
    )
    out_specs = (
        P(("group", "row")),
        P(None, "row", None),
        P(None, "row", None),
        P(),
        P("group", None),
    )
    return jax.shard_map(body, mesh=mesh, in_specs=in_specs, out_specs=out_specs, check_vma=False)
```

profile of v0, /device:TPU:16, one launch (start us, length us, event | category | flops | bytes accessed | tf_op | source)
XLA Modules:
  0.0 299.1 jit_solution(5511135230182900880)
XLA Ops:
  7.2 1.5 pad_maximum_fusion.2
  8.8 1.4 fusion.17
  10.2 0.7 compare_select_fusion
  10.9 8.9 %scatter_custom_fusion = bf16[3072,128]{1,0:T(8,128)(2,1)S(1)} fusion(s32[3072]{0:T(1024)S(1)} %bitcast.121, f32[3072,128]{1,0:T(8,128)} %param.11, f32[128]{0:T(128)S(1)} %get-tuple-element.24, f32[128]{0:T(128)S(1)} %get-tuple-element.23, bf16[]{:T(256)} %constant.1.clone.1), kind=kCustom, calls=%fused_computation.52 | custom fusion | flops 1179648 | bytes 2360322 | tf_op jit(solution)/shard_map/scatter | solution.py:49
  19.9 1.7 convolution_convert_fusion.4
  21.6 11.4 %all-to-all-start = ((bf16[16,192,256]{2,1,0:T(8,128)(2,1)}), bf16[16,192,256]{2,1,0:T(8,128)(2,1)S(1)}, u32[]{:S(2)}, u32[]{:S(2)}) async-start(bf16[16,192,256]{2,1,0:T(8,128)(2,1)} %bitcast.6), calls=%async_computation | async-start | bytes 3145728 | tf_op jit(solution)/shard_map/all_to_all | solution.py:53
  33.0 0.2 reduce-scatter.2.cloned.1.call-start
  33.3 37.7 %all-to-all-done = bf16[16,192,256]{2,1,0:T(8,128)(2,1)S(1)} async-done(((bf16[16,192,256]{2,1,0:T(8,128)(2,1)}), bf16[16,192,256]{2,1,0:T(8,128)(2,1)S(1)}, u32[]{:S(2)}, u32[]{:S(2)}) %all-to-all-start) | async-done | bytes 1572896 | tf_op jit(solution)/shard_map/all_to_all | solution.py:53
  71.0 0.2 copy.47
  71.2 37.0 %all-gather.2.cloned.1.call-done = bf16[4,4096,128]{2,1,0:T(8,128)(2,1)} async-done(((bf16[4,128,128]{2,1,0:T(8,128)(2,1)}), bf16[4,4096,128]{2,1,0:T(8,128)(2,1)}) %all-gather.2.cloned.1.call-update) | async-done | bytes 4194320 | tf_op jit(solution)/shard_map/all_gather | solution.py:57
  108.1 1.8 convolution_convert_fusion.8
  109.9 3.8 %fusion.11 = (bf16[192,4096]{1,0:T(8,128)(2,1)S(1)}, f32[192,4096]{1,0:T(8,128)}) fusion(bf16[192,4096]{1,0:T(8,128)(2,1)S(1)} %bitcast.103, f32[4096]{0:T(1024)S(1)} %bitcast.116, bf16[192,128]{1,0:T(8,128)(2,1)S(1)} %convolution_convert_fusion.8, bf16[4,4096,128]{2,1,0:T(8,128)(2,1)} %all-gather.2.cloned.1.call-done), kind=kOutput, calls=%fused_computation.28 | convolution fusion | flops 205258752 | bytes 7405568 | tf_op jit(solution)/shard_map/dot_general | solution.py:65
  113.7 0.6 convolution_convert_fusion.7
  114.3 2.7 multiply_reduce_fusion
  117.0 0.6 fusion.16
  117.7 0.2 copy.48
  117.8 0.6 convolution_convert_fusion.6
  118.4 0.8 fusion.9
  119.2 2.5 fusion.15
  121.7 0.8 fusion.6
  122.4 0.6 convolution_convert_fusion.5
  123.0 0.8 fusion.8
  123.8 0.8 fusion.7
  124.6 2.2 pad_maximum_fusion
  126.8 4.9 %fusion.5 = bf16[192,4096]{1,0:T(8,128)(2,1)S(1)} fusion(f32[192,4096]{1,0:T(8,128)} %get-tuple-element.29, bf16[192,128]{1,0:T(8,128)(2,1)S(1)} %convolution_convert_fusion.5, f32[192,4096]{1,0:T(8,128)} %get-tuple-element.28, f32[192,4096]{1,0:T(8,128)} %get-tuple-element.26, f32[192]{0:T(256)S(1)} %fusion.26, f32[4096]{0:T(1024)S(1)} %copy-done.5, ...), kind=kOutput, calls=%fused_computation.15 | convolution fusion | flops 209977344 | bytes 12124928 | tf_op jit(solution)/shard_map/dot_general | solution.py:95
  131.8 1.3 copy.55
  133.1 7.5 %all-to-all-start.1 = ((bf16[192,16,256]{2,0,1:T(8,128)(2,1)}), bf16[192,16,256]{2,0,1:T(8,128)(2,1)}, u32[]{:S(2)}, u32[]{:S(2)}) async-start(bf16[192,16,256]{2,0,1:T(8,128)(2,1)} %bitcast.108), calls=%async_computation.2 | async-start | bytes 3145728 | tf_op jit(solution)/shard_map/all_to_all | solution.py:106
  140.6 0.5 convert_reduce_fusion
  141.2 38.0 %all-to-all-done.1 = bf16[192,16,256]{2,0,1:T(8,128)(2,1)} async-done(((bf16[192,16,256]{2,0,1:T(8,128)(2,1)}), bf16[192,16,256]{2,0,1:T(8,128)(2,1)}, u32[]{:S(2)}, u32[]{:S(2)}) %all-to-all-start.1) | async-done | bytes 1572896 | tf_op jit(solution)/shard_map/all_to_all | solution.py:106
  179.1 2.1 fusion.29
  181.3 0.1 all_to_all.64
  181.4 18.1 %all_to_all.81 = f32[32,1,1280]{2,1,0:T(1,128)S(1)} all-to-all(f32[32,1,1280]{2,1,0:T(1,128)S(1)} %all_to_all.64), channel_id=1, replica_groups=mesh['group'=16,'row'=32] {'row'}, dimensions={0} | all-to-all | bytes 327680 | tf_op jit(solution)/shard_map/all_to_all | solution.py:117
  199.5 0.1 reduce_sum.60
  199.6 0.1 all_to_all.66
  199.7 13.0 %all_to_all.82 = f32[16,1,16]{2,1,0:T(1,128)S(1)} all-to-all(f32[16,1,16]{2,1,0:T(1,128)S(1)} %all_to_all.66), channel_id=1, replica_groups=mesh['group'=16,'row'=32] {'group'}, dimensions={0} | all-to-all | bytes 2048 | tf_op jit(solution)/shard_map/all_to_all | solution.py:15
  212.7 0.6 broadcast_in_dim.9
  213.3 3.5 %all-to-all-start.4 = ((f32[16,1,16]{2,1,0:T(1,128)}), f32[16,1,16]{2,1,0:T(1,128)S(1)}, u32[]{:S(2)}, u32[]{:S(2)}) async-start(f32[16,1,16]{2,1,0:T(1,128)} %broadcast_in_dim.9), calls=%async_computation.5 | async-start | bytes 16384 | tf_op jit(solution)/shard_map/all_to_all | solution.py:17
  216.8 8.3 %all-to-all-done.4 = f32[16,1,16]{2,1,0:T(1,128)S(1)} async-done(((f32[16,1,16]{2,1,0:T(1,128)}), f32[16,1,16]{2,1,0:T(1,128)S(1)}, u32[]{:S(2)}, u32[]{:S(2)}) %all-to-all-start.4) | async-done | bytes 1056 | tf_op jit(solution)/shard_map/all_to_all | solution.py:17
  225.1 0.5 broadcast.39
  225.6 0.7 reduce.6
  226.5 15.9 %all_to_all.83 = f32[32,1,1280]{2,1,0:T(1,128)S(1)} all-to-all(f32[32,1,1280]{2,1,0:T(1,128)S(1)} %broadcast_in_dim.10), channel_id=1, replica_groups=mesh['group'=16,'row'=32] {'row'}, dimensions={0} | all-to-all | bytes 327680 | tf_op jit(solution)/shard_map/all_to_all | solution.py:124
  242.4 0.7 reshape.118
  243.1 0.6 reshape.119
  243.8 19.4 %reduce-scatter.2.cloned.1.call-done = bf16[4,128,128]{2,1,0:T(8,128)(2,1)} async-done(((bf16[4,4096,128]{2,1,0:T(8,128)(2,1)}), bf16[4,128,128]{2,1,0:T(8,128)(2,1)}) %reduce-scatter.2.cloned.1.call-update) | async-done | bytes 131088 | tf_op jit(solution)/shard_map/reduce_scatter | solution.py:104
  263.2 0.9 copy_bitcast_fusion.2
  264.1 15.7 %all_to_all.84 = bf16[16,4,8,128]{3,2,1,0:T(8,128)(2,1)S(1)} all-to-all(bf16[16,4,8,128]{3,2,1,0:T(8,128)(2,1)S(1)} %copy_bitcast_fusion.2), channel_id=1, replica_groups=mesh['group'=16,'row'=32] {'group'}, dimensions={0} | all-to-all | bytes 262144 | tf_op jit(solution)/shard_map/all_to_all | solution.py:23
  279.9 11.6 %all_to_all.85 = bf16[16,4,8,128]{3,2,1,0:T(8,128)(2,1)S(1)} all-to-all(bf16[16,4,8,128]{3,2,1,0:T(8,128)(2,1)S(1)} %broadcast_in_dim.11), channel_id=1, replica_groups=mesh['group'=16,'row'=32] {'group'}, dimensions={0} | all-to-all | bytes 262144 | tf_op jit(solution)/shard_map/all_to_all | solution.py:25
  291.5 0.7 slice_bitcast_fusion.12
  (41 shorter events, 0.5 us)
Async XLA Ops:
  7.2 12.7 %copy-start = (bf16[128,256]{1,0:T(8,128)(2,1)S(1)}, bf16[128,256]{1,0:T(8,128)(2,1)}, u32[]{:S(2)}) copy-start(bf16[128,256]{1,0:T(8,128)(2,1)} %param.15) | copy-start | bytes 196612
  7.2 101.0 %all-gather.2.cloned.1.call-start = ((), (), s32[]{:S(2)}) async-start(), calls=%async_computation.9 | async-start | bytes 4325376 | tf_op jit(solution)/shard_map/all_gather | solution.py:57
  19.8 1.8 copy-start.3
  19.8 13.3 %copy-start.5 = (f32[4096]{0:T(1024)S(1)}, f32[4096]{0:T(1024)}, u32[]{:S(2)}) copy-start(f32[4096]{0:T(1024)} %param.20) | copy-start | bytes 49156
  19.8 13.4 %copy-start.6 = (f32[2,4096]{1,0:T(2,128)S(1)}, f32[2,4096]{1,0:T(2,128)}, u32[]{:S(2)}) copy-start(f32[2,4096]{1,0:T(2,128)} %param.19) | copy-start | bytes 98308
  21.6 49.4 %all-to-all-start = ((bf16[16,192,256]{2,1,0:T(8,128)(2,1)}), bf16[16,192,256]{2,1,0:T(8,128)(2,1)S(1)}, u32[]{:S(2)}, u32[]{:S(2)}) async-start(bf16[16,192,256]{2,1,0:T(8,128)(2,1)} %bitcast.6), calls=%async_computation | async-start | bytes 3145728 | tf_op jit(solution)/shard_map/all_to_all | solution.py:53
  33.0 230.2 %reduce-scatter.2.cloned.1.call-start = ((), (), s32[]{:S(2)}) async-start(), calls=%async_computation.10 | async-start | bytes 4325376 | tf_op jit(solution)/shard_map/reduce_scatter | solution.py:104
  109.9 3.8 %copy-start.4 = (bf16[4,4096,128]{2,1,0:T(8,128)(2,1)S(1)}, bf16[4,4096,128]{2,1,0:T(8,128)(2,1)}, u32[]{:S(2)}) copy-start(bf16[4,4096,128]{2,1,0:T(8,128)(2,1)} %all-gather.2.cloned.1.call-done) | copy-start | bytes 12582916
  114.3 2.7 copy-start.8
  117.0 0.8 copy-start.7
  121.7 2.1 copy-start.1
  131.7 8.9 %copy-start.2 = (bf16[192,4096]{1,0:T(8,128)(2,1)S(1)}, bf16[192,4096]{1,0:T(8,128)(2,1)}, u32[]{:S(2)}) copy-start(bf16[192,4096]{1,0:T(8,128)(2,1)} %copy-done.1) | copy-start | bytes 4718596
  133.1 46.0 %all-to-all-start.1 = ((bf16[192,16,256]{2,0,1:T(8,128)(2,1)}), bf16[192,16,256]{2,0,1:T(8,128)(2,1)}, u32[]{:S(2)}, u32[]{:S(2)}) async-start(bf16[192,16,256]{2,0,1:T(8,128)(2,1)} %bitcast.108), calls=%async_computation.2 | async-start | bytes 3145728 | tf_op jit(solution)/shard_map/all_to_all | solution.py:106
  213.3 11.8 %all-to-all-start.4 = ((f32[16,1,16]{2,1,0:T(1,128)}), f32[16,1,16]{2,1,0:T(1,128)S(1)}, u32[]{:S(2)}, u32[]{:S(2)}) async-start(f32[16,1,16]{2,1,0:T(1,128)} %broadcast_in_dim.9), calls=%async_computation.5 | async-start | bytes 16384 | tf_op jit(solution)/shard_map/all_to_all | solution.py:17
Sparse Core Ops, SparseCore 0:
  12.0 96.0 all-gather.1
  127.0 136.1 reduce-scatter.1
where the time goes:
time: 300 us; the launch traced here: 299 us
  waiting for transfers between devices  140 us (47%)
  blocking collectives  74.3 us (25%)
  matrix products  25.6 us (9%)
  starting transfers between devices  22.6 us (8%)
  other arithmetic  15.4 us (5%)
  between operations  14.4 us (5%)
  local copies, waits for them, and re-layouts  6.32 us (2%)
    all_to_all x1, waiting for transfers between devices, body(): lax.all_to_all(first_grad, 'group', split_axis=1, concat_axis=0, tiled=True)  38 us
    all_to_all x1, waiting for transfers between devices, body(): lax.all_to_all(projected, 'group', split_axis=0, concat_axis=1, tiled=True)  37.7 us
    all_gather x1, waiting for transfers between devices, body(): lax.all_gather(jnp.concatenate([down_weight, up_weight], axis=0), 'row',...  37 us
    reduce_scatter x1, waiting for transfers between devices, body(): weight_rows = lax.psum_scatter(slab, 'row', scatter_dimension=1, tiled=True)  19.4 us
    all_to_all x1, blocking collectives, body(): lax.all_to_all(jnp.concatenate([proj_pieces, bias_pieces], axis=1), 'row'...  18.1 us
    all_to_all x1, blocking collectives, body(): lax.all_to_all(jnp.broadcast_to(last[None], (row_count_axis,) + last.shap...  15.9 us
    all_to_all x1, blocking collectives, group_all_reduce(): lax.all_to_all(pieces, 'group', 0, 0, tiled=True).astype(jnp.float32)  15.7 us
    all_to_all x1, blocking collectives, exchange_sum(): mine = jnp.sum(lax.all_to_all(pieces, axis, 0, 0, tiled=True), axis=0)  13 us
  transfers between devices with their start and end apart: 5, of which 5 were waited for; matrix products, arithmetic and copies ran while one was open for 8% of the time, Pallas kernels for 0%

commit v1 on v0

--- a/solution.py
+++ b/solution.py
@@ -54,9 +54,11 @@
     first_wide = first.astype(jnp.float32)
     crossed = first
     stored = []
-    weights_full = lax.all_gather(
-        jnp.concatenate([down_weight, up_weight], axis=0), "row", axis=1, tiled=True
-    )
+    own = jnp.concatenate([down_weight, up_weight], axis=0)
+    size = lax.axis_size("row")
+    shards = jnp.stack([own for _ in range(size)])
+    shards = lax.all_to_all(shards, "row", split_axis=0, concat_axis=0)
+    weights_full = jnp.concatenate(shards, axis=1)
     for layer_index in range(layers):
         down_full, up_full = (weights_full[layer_index], weights_full[layers + layer_index])
         hidden = jnp.dot(crossed, down_full, preferred_element_type=jnp.float32).astype(

time: 300 us -> 367 us (1.22)
  waiting for transfers between devices: 140 us -> 195 us
  starting transfers between devices: 22.6 us -> 29.6 us
  local copies, waits for them, and re-layouts: 6.32 us -> 13.3 us
    all_to_all x0 -> x1, waiting for transfers between devices: none -> 92.1 us  [body(): shards = lax.all_to_all(shards, 'row', split_axis=0, concat_axis=0)]
    all_gather x1 -> x0, waiting for transfers between devices: 37 us -> none  [body(): lax.all_gather(jnp.concatenate([down_weight, up_weight], axis=0), 'row',...]
    all_to_all x0 -> x1, starting transfers between devices: none -> 9.95 us  [body(): shards = lax.all_to_all(shards, 'row', split_axis=0, concat_axis=0)]
  transfers between devices with their start and end apart: 5 -> 5, of which waited for: 5 -> 5; matrix products, arithmetic and copies ran while one was open for 8% -> 3% of each run, Pallas kernels for 0% -> 0%
where the time goes in v1:
time: 367 us; the launch traced here: 366 us
  waiting for transfers between devices  195 us (53%)
  blocking collectives  77.8 us (21%)
  starting transfers between devices  29.6 us (8%)
  matrix products  22.7 us (6%)
  between operations  14.4 us (4%)
  other arithmetic  13.9 us (4%)
  local copies, waits for them, and re-layouts  13.3 us (4%)
    all_to_all x1, waiting for transfers between devices, body(): shards = lax.all_to_all(shards, 'row', split_axis=0, concat_axis=0)  92.1 us
    all_to_all x1, waiting for transfers between devices, body(): lax.all_to_all(projected, 'group', split_axis=0, concat_axis=1, tiled=True)  38 us
    all_to_all x1, waiting for transfers between devices, body(): lax.all_to_all(first_grad, 'group', split_axis=1, concat_axis=0, tiled=True)  37.2 us
    all_to_all x1, blocking collectives, body(): lax.all_to_all(jnp.concatenate([proj_pieces, bias_pieces], axis=1), 'row'...  21.3 us
    reduce_scatter x1, waiting for transfers between devices, body(): weight_rows = lax.psum_scatter(slab, 'row', scatter_dimension=1, tiled=True)  18.9 us
    all_to_all x1, blocking collectives, body(): lax.all_to_all(jnp.broadcast_to(last[None], (row_count_axis,) + last.shap...  16.1 us
    all_to_all x1, blocking collectives, group_all_reduce(): lax.all_to_all(pieces, 'group', 0, 0, tiled=True).astype(jnp.float32)  15.9 us
    all_to_all x1, blocking collectives, exchange_sum(): mine = jnp.sum(lax.all_to_all(pieces, axis, 0, 0, tiled=True), axis=0)  12.9 us
  transfers between devices with their start and end apart: 5, of which 5 were waited for; matrix products, arithmetic and copies ran while one was open for 3% of the time, Pallas kernels for 0%

profile of v1, /device:TPU:16, one launch (start us, length us, event | category | flops | bytes accessed | tf_op | source)
XLA Modules:
  0.0 366.3 jit_solution(816247132235613609)
XLA Ops:
  7.2 1.4 fusion.17
  8.6 0.7 compare_select_fusion
  9.3 8.9 %scatter_custom_fusion = bf16[3072,128]{1,0:T(8,128)(2,1)S(1)} fusion(s32[3072]{0:T(1024)S(1)} %bitcast.120, f32[3072,128]{1,0:T(8,128)} %param.11, f32[128]{0:T(128)S(1)} %get-tuple-element.28, f32[128]{0:T(128)S(1)} %get-tuple-element.27, bf16[]{:T(256)} %constant.1.clone.1), kind=kCustom, calls=%fused_computation.48 | custom fusion | flops 1179648 | bytes 2360322 | tf_op jit(solution)/shard_map/scatter | solution.py:49
  18.3 1.7 convolution_convert_fusion.4
  20.0 11.5 %all-to-all-start = ((bf16[16,192,256]{2,1,0:T(8,128)(2,1)}), bf16[16,192,256]{2,1,0:T(8,128)(2,1)S(1)}, u32[]{:S(2)}, u32[]{:S(2)}) async-start(bf16[16,192,256]{2,1,0:T(8,128)(2,1)} %bitcast.6), calls=%async_computation | async-start | bytes 3145728 | tf_op jit(solution)/shard_map/all_to_all | solution.py:53
  31.5 38.0 %all-to-all-done = bf16[16,192,256]{2,1,0:T(8,128)(2,1)S(1)} async-done(((bf16[16,192,256]{2,1,0:T(8,128)(2,1)}), bf16[16,192,256]{2,1,0:T(8,128)(2,1)S(1)}, u32[]{:S(2)}, u32[]{:S(2)}) %all-to-all-start) | async-done | bytes 1572896 | tf_op jit(solution)/shard_map/all_to_all | solution.py:53
  69.5 3.0 stack.32
  72.5 10.0 %all-to-all-start.1 = ((bf16[32,4,128,128]{3,2,1,0:T(8,128)(2,1)}), bf16[32,4,128,128]{3,2,1,0:T(8,128)(2,1)}, u32[]{:S(2)}, u32[]{:S(2)}) async-start(bf16[32,4,128,128]{3,2,1,0:T(8,128)(2,1)} %stack.32), calls=%async_computation.1 | async-start | bytes 8388608 | tf_op jit(solution)/shard_map/all_to_all | solution.py:60
  82.5 0.2 reduce-scatter.2.cloned.1.call-start
  82.8 0.2 copy.47
  83.0 92.1 %all-to-all-done.1 = bf16[32,4,128,128]{3,2,1,0:T(8,128)(2,1)} async-done(((bf16[32,4,128,128]{3,2,1,0:T(8,128)(2,1)}), bf16[32,4,128,128]{3,2,1,0:T(8,128)(2,1)}, u32[]{:S(2)}, u32[]{:S(2)}) %all-to-all-start.1) | async-done | bytes 4194336 | tf_op jit(solution)/shard_map/all_to_all | solution.py:60
  175.0 2.8 fusion.28
  177.8 0.6 convolution_convert_fusion.8
  178.4 2.4 fusion.11
  180.7 0.6 convolution_convert_fusion.7
  181.3 2.7 multiply_reduce_fusion
  184.0 0.6 fusion.16
  184.6 0.2 copy.48
  184.8 0.6 convolution_convert_fusion.6
  185.4 0.8 fusion.9
  186.2 2.6 fusion.15
  188.8 0.6 convolution_convert_fusion.5
  189.3 0.8 fusion.6
  190.1 0.8 fusion.8
  190.9 0.8 fusion.7
  191.7 2.2 pad_maximum_fusion
  193.9 1.2 copy-done.4
  195.1 4.6 %fusion.5 = bf16[192,4096]{1,0:T(8,128)(2,1)S(1)} fusion(f32[192,4096]{1,0:T(8,128)} %get-tuple-element.33, bf16[192,128]{1,0:T(8,128)(2,1)S(1)} %convolution_convert_fusion.5, bf16[4096,128]{1,0:T(8,128)(2,1)S(1)} %bitcast.100, f32[192,4096]{1,0:T(8,128)} %get-tuple-element.32, f32[192,4096]{1,0:T(8,128)} %get-tuple-element.30, f32[192]{0:T(256)S(1)} %fusion.26, ...), kind=kOutput, calls=%fused_computation.15 | convolution fusion | flops 209977344 | bytes 12124928 | tf_op jit(solution)/shard_map/dot_general | solution.py:97
  199.7 1.3 copy.55
  201.1 4.5 %all-to-all-start.2 = ((bf16[192,16,256]{2,0,1:T(8,128)(2,1)}), bf16[192,16,256]{2,0,1:T(8,128)(2,1)}, u32[]{:S(2)}, u32[]{:S(2)}) async-start(bf16[192,16,256]{2,0,1:T(8,128)(2,1)} %bitcast.107), calls=%async_computation.3 | async-start | bytes 3145728 | tf_op jit(solution)/shard_map/all_to_all | solution.py:108
  205.6 0.5 convert_reduce_fusion
  206.2 37.2 %all-to-all-done.2 = bf16[192,16,256]{2,0,1:T(8,128)(2,1)} async-done(((bf16[192,16,256]{2,0,1:T(8,128)(2,1)}), bf16[192,16,256]{2,0,1:T(8,128)(2,1)}, u32[]{:S(2)}, u32[]{:S(2)}) %all-to-all-start.2) | async-done | bytes 1572896 | tf_op jit(solution)/shard_map/all_to_all | solution.py:108
  243.4 2.1 fusion.30
  245.7 21.3 %all_to_all.86 = f32[32,1,1280]{2,1,0:T(1,128)S(1)} all-to-all(f32[32,1,1280]{2,1,0:T(1,128)S(1)} %all_to_all.68), channel_id=1, replica_groups=mesh['group'=16,'row'=32] {'row'}, dimensions={0} | all-to-all | bytes 327680 | tf_op jit(solution)/shard_map/all_to_all | solution.py:119
  267.2 12.9 %all_to_all.87 = f32[16,1,16]{2,1,0:T(1,128)S(1)} all-to-all(f32[16,1,16]{2,1,0:T(1,128)S(1)} %all_to_all.70), channel_id=1, replica_groups=mesh['group'=16,'row'=32] {'group'}, dimensions={0} | all-to-all | bytes 2048 | tf_op jit(solution)/shard_map/all_to_all | solution.py:15
  280.1 0.6 broadcast_in_dim.9
  280.7 3.5 all-to-all-start.5
  284.2 8.3 %all-to-all-done.5 = f32[16,1,16]{2,1,0:T(1,128)S(1)} async-done(((f32[16,1,16]{2,1,0:T(1,128)}), f32[16,1,16]{2,1,0:T(1,128)S(1)}, u32[]{:S(2)}, u32[]{:S(2)}) %all-to-all-start.5) | async-done | bytes 1056 | tf_op jit(solution)/shard_map/all_to_all | solution.py:17
  292.5 0.5 broadcast.41
  293.1 0.7 reduce.6
  293.9 16.1 %all_to_all.88 = f32[32,1,1280]{2,1,0:T(1,128)S(1)} all-to-all(f32[32,1,1280]{2,1,0:T(1,128)S(1)} %broadcast_in_dim.10), channel_id=1, replica_groups=mesh['group'=16,'row'=32] {'row'}, dimensions={0} | all-to-all | bytes 327680 | tf_op jit(solution)/shard_map/all_to_all | solution.py:126
  310.0 0.7 reshape.133
  310.7 0.6 reshape.134
  311.4 18.9 %reduce-scatter.2.cloned.1.call-done = bf16[4,128,128]{2,1,0:T(8,128)(2,1)} async-done(((bf16[4,4096,128]{2,1,0:T(8,128)(2,1)}), bf16[4,128,128]{2,1,0:T(8,128)(2,1)}) %reduce-scatter.2.cloned.1.call-update) | async-done | bytes 131088 | tf_op jit(solution)/shard_map/reduce_scatter | solution.py:106
  330.2 0.9 copy_bitcast_fusion.2
  331.2 15.9 %all_to_all.89 = bf16[16,4,8,128]{3,2,1,0:T(8,128)(2,1)S(1)} all-to-all(bf16[16,4,8,128]{3,2,1,0:T(8,128)(2,1)S(1)} %copy_bitcast_fusion.2), channel_id=1, replica_groups=mesh['group'=16,'row'=32] {'group'}, dimensions={0} | all-to-all | bytes 262144 | tf_op jit(solution)/shard_map/all_to_all | solution.py:23
  347.1 11.6 %all_to_all.90 = bf16[16,4,8,128]{3,2,1,0:T(8,128)(2,1)S(1)} all-to-all(bf16[16,4,8,128]{3,2,1,0:T(8,128)(2,1)S(1)} %broadcast_in_dim.11), channel_id=1, replica_groups=mesh['group'=16,'row'=32] {'group'}, dimensions={0} | all-to-all | bytes 262144 | tf_op jit(solution)/shard_map/all_to_all | solution.py:25
  358.8 0.7 slice_bitcast_fusion
  (48 shorter events, 0.8 us)
Async XLA Ops:
  7.2 11.1 %copy-start = (bf16[128,256]{1,0:T(8,128)(2,1)S(1)}, bf16[128,256]{1,0:T(8,128)(2,1)}, u32[]{:S(2)}) copy-start(bf16[128,256]{1,0:T(8,128)(2,1)} %param.15) | copy-start | bytes 196612
  18.2 1.7 copy-start.5
  20.0 11.5 %copy-start.7 = (bf16[2,128,128]{2,1,0:T(8,128)(2,1)S(1)}, bf16[2,128,128]{2,1,0:T(8,128)(2,1)}, u32[]{:S(2)}) copy-start(bf16[2,128,128]{2,1,0:T(8,128)(2,1)} %param.18) | copy-start | bytes 196612
  20.0 11.5 %copy-start.8 = (bf16[2,128,128]{2,1,0:T(8,128)(2,1)S(1)}, bf16[2,128,128]{2,1,0:T(8,128)(2,1)}, u32[]{:S(2)}) copy-start(bf16[2,128,128]{2,1,0:T(8,128)(2,1)} %param.17) | copy-start | bytes 196612
  20.0 49.5 %all-to-all-start = ((bf16[16,192,256]{2,1,0:T(8,128)(2,1)}), bf16[16,192,256]{2,1,0:T(8,128)(2,1)S(1)}, u32[]{:S(2)}, u32[]{:S(2)}) async-start(bf16[16,192,256]{2,1,0:T(8,128)(2,1)} %bitcast.6), calls=%async_computation | async-start | bytes 3145728 | tf_op jit(solution)/shard_map/all_to_all | solution.py:53
  72.5 10.2 %copy-start.6 = (f32[4096]{0:T(1024)S(1)}, f32[4096]{0:T(1024)}, u32[]{:S(2)}) copy-start(f32[4096]{0:T(1024)} %param.20) | copy-start | bytes 49156
  72.5 10.2 %copy-start.9 = (f32[2,4096]{1,0:T(2,128)S(1)}, f32[2,4096]{1,0:T(2,128)}, u32[]{:S(2)}) copy-start(f32[2,4096]{1,0:T(2,128)} %param.19) | copy-start | bytes 98308
  72.5 102.5 %all-to-all-start.1 = ((bf16[32,4,128,128]{3,2,1,0:T(8,128)(2,1)}), bf16[32,4,128,128]{3,2,1,0:T(8,128)(2,1)}, u32[]{:S(2)}, u32[]{:S(2)}) async-start(bf16[32,4,128,128]{3,2,1,0:T(8,128)(2,1)} %stack.32), calls=%async_computation.1 | async-start | bytes 8388608 | tf_op jit(solution)/shard_map/all_to_all | solution.py:60
  82.5 247.8 %reduce-scatter.2.cloned.1.call-start = ((), (), s32[]{:S(2)}) async-start(), calls=%async_computation.10 | async-start | bytes 4325376 | tf_op jit(solution)/shard_map/reduce_scatter | solution.py:106
  177.8 2.9 copy-start.3
  181.3 2.7 copy-start.11
  184.0 0.8 copy-start.10
  188.8 2.1 copy-start.1
  193.9 1.2 copy-start.4
  201.1 4.5 %copy-start.2 = (bf16[192,4096]{1,0:T(8,128)(2,1)S(1)}, bf16[192,4096]{1,0:T(8,128)(2,1)}, u32[]{:S(2)}) copy-start(bf16[192,4096]{1,0:T(8,128)(2,1)} %copy-done.1) | copy-start | bytes 4718596
  201.1 42.3 %all-to-all-start.2 = ((bf16[192,16,256]{2,0,1:T(8,128)(2,1)}), bf16[192,16,256]{2,0,1:T(8,128)(2,1)}, u32[]{:S(2)}, u32[]{:S(2)}) async-start(bf16[192,16,256]{2,0,1:T(8,128)(2,1)} %bitcast.107), calls=%async_computation.3 | async-start | bytes 3145728 | tf_op jit(solution)/shard_map/all_to_all | solution.py:108
  280.7 11.8 %all-to-all-start.5 = ((f32[16,1,16]{2,1,0:T(1,128)}), f32[16,1,16]{2,1,0:T(1,128)S(1)}, u32[]{:S(2)}, u32[]{:S(2)}) async-start(f32[16,1,16]{2,1,0:T(1,128)} %broadcast_in_dim.9), calls=%async_computation.6 | async-start | bytes 16384 | tf_op jit(solution)/shard_map/all_to_all | solution.py:17
Sparse Core Ops, SparseCore 0:
  194.1 136.1 reduce-scatter.1
